TPU v7x, 256 devices: a whole 4x4x8 slice. The times are simulated.
256 devices in a mesh: ctx: 8 (over x, z_lo), tp: 32 (over z_hi, y, core).
Axes of the slice: x: 4, y: 4, z: 8 (z_hi: 4, z_lo: 2; z = z_hi * 2 + z_lo), core: 2. Of those that a mesh axis runs over, the one named last changes fastest.
Arguments:
- states: bfloat16 [8192, 2048], P(('ctx', 'tp')), may hold values from -6 to 6
- short_lengths: int32 [64], P('ctx'), may hold values from 1 to 64, 3072 in all
- attn_gain: float32 [2048], replicated, may hold values from 0.5 to 16
- wq: bfloat16 [2048, 2048], P(None, 'tp'), may hold values from -0.125 to 0.125
- wkv: bfloat16 [2048, 512], replicated, may hold values from -0.125 to 0.125
- wo: bfloat16 [2048, 2048], P('tp'), may hold values from -0.125 to 0.125
- mlp_gain: float32 [2048], replicated, may hold values from 0.5 to 1.5
- w_gate: bfloat16 [2048, 5632], P(None, 'tp'), may hold values from -0.125 to 0.125
- w_up: bfloat16 [2048, 5632], P(None, 'tp'), may hold values from -0.125 to 0.125
- w_down: bfloat16 [5632, 2048], P('tp'), may hold values from -0.078125 to 0.078125
Outputs:
- updated: bfloat16 [8192, 2048], P(('ctx', 'tp'))
- long_cache: bfloat16 [2, 2048, 512], P(None, 'ctx', 'tp')
- short_cache: bfloat16 [64, 64, 512], P('ctx', None, 'tp')
Inputs may be any that keep to these rules, and one draw needn't show every extreme that they name: `short_lengths`: rows of a short prompt at or beyond its length are padding; the largest length is 64.
All inputs are finite; a program needn't handle non-finite values. No bound on the sum of `short_lengths` on one device may be relied on, other than what follows from the above.
Results may differ from a plain program's by a relative error of at most 0.022.
The roundings to bfloat16 on the way count: a program that leaves them out, or rounds other values in their place, can miss the bound.
Values may be sent and summed in bfloat16 or wider, within the bound.
No kernel may reach another device: no remote copies, remote signals or barrier semaphores. Data moves between devices by JAX's collectives and lax.ppermute only.
A program may use at most 64 MiB of HBM per device.

v0:
```python
import jax
import jax.numpy as jnp
from jax import lax
from jax.sharding import PartitionSpec as P

KVH = 4
HEAD_SIZE = 64
LONG = 2
LLEN = 2048
SLEN = 64
EPS = 1e-05
THETA = 10000.0
NEG = -1e30


def rms_scale(matrix, gain):
    entries = matrix.astype(jnp.float32)
    power = jnp.mean(entries * entries, axis=-1, keepdims=True)
    return (entries * lax.rsqrt(power + EPS) * gain).astype(jnp.bfloat16)


def rotate(entries, positions):
    half_width = entries.shape[-1] // 2
    frequency = THETA ** (-jnp.arange(half_width, dtype=jnp.float32) * 2.0 / entries.shape[-1])
    angles = positions.astype(jnp.float32)[:, None] * frequency[None, :]
    cosine = jnp.cos(angles)[:, None, :]
    sine_wave = jnp.sin(angles)[:, None, :]
    first_half = entries[..., :half_width]
    second_half = entries[..., half_width:]
    return jnp.concatenate(
        [
            first_half * cosine - second_half * sine_wave,
            second_half * cosine + first_half * sine_wave,
        ],
        axis=-1,
    )


def rank_positions(ctx_rank, rank_rows, block_len, long_rows, n_blocks):
    index_row = jnp.arange(rank_rows, dtype=jnp.int32)
    half_index = index_row // block_len % 2
    offset_row = index_row % block_len
    which_block = jnp.where(half_index == 0, ctx_rank, n_blocks - 1 - ctx_rank)
    long_pos = which_block * block_len + offset_row
    short_pos = (index_row - long_rows) % SLEN
    return jnp.where(index_row < long_rows, long_pos, short_pos)


def project(matrix, positions, wq, wkv_head, heads_dev):
    row_count = matrix.shape[0]
    query_matrix = jnp.dot(matrix, wq, preferred_element_type=jnp.float32).reshape(
        row_count, heads_dev, HEAD_SIZE
    )
    query_matrix = rotate(query_matrix, positions).astype(jnp.bfloat16)
    pairs = jnp.dot(matrix, wkv_head, preferred_element_type=jnp.float32)
    key_matrix = rotate(pairs[:, None, :HEAD_SIZE], positions).astype(jnp.bfloat16)[:, 0]
    value_matrix = pairs[:, HEAD_SIZE:].astype(jnp.bfloat16)
    return jnp.concatenate(
        [query_matrix.reshape(row_count, heads_dev * HEAD_SIZE), key_matrix, value_matrix], axis=1
    )


def attend(soft_state, query_matrix, query_pos, key_matrix, value_matrix, key_pos, valid_keys):
    best_score, weight_sum, weighted = soft_state
    logit_scores = jnp.einsum(
        "rzsm,rvm->rzsv", query_matrix, key_matrix, preferred_element_type=jnp.float32
    ) * HEAD_SIZE ** (-0.5)
    allowed = (key_pos[None, :] <= query_pos[:, None])[None, None] & valid_keys[:, None, None, :]
    logit_scores = jnp.where(allowed, logit_scores, NEG)
    new_best = jnp.maximum(best_score, jnp.max(logit_scores, axis=-1))
    weights = jnp.where(allowed, jnp.exp(logit_scores - new_best[..., None]), 0.0)
    weight_sum = jnp.sum(weights, axis=-1)
    weighted = jnp.einsum(
        "awlp,ape->awle",
        weights.astype(jnp.bfloat16),
        value_matrix,
        preferred_element_type=jnp.float32,
    )
    return (new_best, weight_sum, weighted)


def per_device(states, short_lengths, attn_gain, wq, wkv, wo, mlp_gain, w_gate, w_up, w_down):
    n_ctx = lax.axis_size("ctx")
    n_tp = lax.axis_size("tp")
    ctx_rank = lax.axis_index("ctx")
    tp_index = lax.axis_index("tp")
    tok_rows = states.shape[0]
    rank_rows = tok_rows * n_tp
    n_blocks = 2 * n_ctx
    block_len = LLEN // n_blocks
    long_rows = LONG * 2 * block_len
    heads_dev = wq.shape[1] // HEAD_SIZE
    q_cols = heads_dev * HEAD_SIZE
    pair_width = 2 * HEAD_SIZE
    cache_cols = KVH * pair_width // n_tp
    kv_group = tp_index * KVH // n_tp
    wkv_head = lax.dynamic_slice_in_dim(wkv, kv_group * pair_width, pair_width, 1)
    first_col = tp_index * cache_cols - kv_group * pair_width
    positions = rank_positions(ctx_rank, rank_rows, block_len, long_rows, n_blocks)
    packed = project(
        lax.all_gather(rms_scale(states, attn_gain), "tp", axis=0, tiled=True),
        positions,
        wq,
        wkv_head,
        heads_dev,
    )
    query_matrix = packed[:, :q_cols].reshape(rank_rows, heads_dev, HEAD_SIZE)
    key_matrix = packed[:, q_cols : q_cols + HEAD_SIZE]
    value_matrix = packed[:, q_cols + HEAD_SIZE :]
    long_q = (
        query_matrix[:long_rows]
        .reshape(LONG, 2 * block_len, heads_dev, HEAD_SIZE)
        .transpose(0, 2, 1, 3)
    )
    long_k = key_matrix[:long_rows].reshape(LONG, 2, 1, block_len, HEAD_SIZE)
    long_v = value_matrix[:long_rows].reshape(LONG, 2, 1, block_len, HEAD_SIZE)
    long_qpos = positions[: 2 * block_len]
    half_pick = jnp.arange(2, dtype=jnp.int32)[:, None, None]
    long_init = (
        jnp.full((LONG, heads_dev, 2 * block_len), NEG, jnp.float32),
        jnp.zeros((LONG, heads_dev, 2 * block_len), jnp.float32),
        jnp.zeros((LONG, heads_dev, 2 * block_len, HEAD_SIZE), jnp.float32),
        jnp.zeros((LONG, 2, block_len, cache_cols), jnp.float32),
    )
    piece_k = lax.all_gather(long_k, "ctx", axis=2, tiled=True)
    piece_v = lax.all_gather(long_v, "ctx", axis=2, tiled=True)
    piece_blocks = piece_k.shape[2]
    block_ids = jnp.arange(piece_blocks, dtype=jnp.int32)
    held_blocks = jnp.stack([block_ids, n_blocks - 1 - block_ids])
    key_pos = (
        held_blocks[:, :, None] * block_len + jnp.arange(block_len, dtype=jnp.int32)
    ).reshape(-1)
    key_count = 2 * piece_blocks * block_len
    flat_k = piece_k.reshape(LONG, key_count, HEAD_SIZE)
    flat_v = piece_v.reshape(LONG, key_count, HEAD_SIZE)
    all_valid = jnp.ones((LONG, key_count), dtype=bool)
    soft_state = long_init[:3]
    soft_state = attend(soft_state, long_q, long_qpos, flat_k, flat_v, key_pos, all_valid)
    joined = jnp.concatenate([piece_k, piece_v], axis=-1)
    own_cols = lax.dynamic_slice_in_dim(joined, first_col, cache_cols, 4)
    selector = ((held_blocks[None] // 2 == ctx_rank) & (held_blocks[None] % 2 == half_pick)).astype(
        jnp.bfloat16
    )
    cache_rows = jnp.einsum(
        "ehj,phjbc->pebc", selector, own_cols, preferred_element_type=jnp.float32
    )
    folded = soft_state + (cache_rows,)
    long_out = (
        (folded[2] / folded[1][..., None])
        .astype(jnp.bfloat16)
        .transpose(0, 2, 1, 3)
        .reshape(long_rows, q_cols)
    )
    long_cache = folded[3].astype(jnp.bfloat16).reshape(LONG, 2 * block_len, cache_cols)
    short_count = short_lengths.shape[0]
    short_q = (
        query_matrix[long_rows:]
        .reshape(short_count, SLEN, heads_dev, HEAD_SIZE)
        .transpose(0, 2, 1, 3)
    )
    short_k = key_matrix[long_rows:].reshape(short_count, SLEN, HEAD_SIZE)
    short_v = value_matrix[long_rows:].reshape(short_count, SLEN, HEAD_SIZE)
    offsets = jnp.arange(SLEN, dtype=jnp.int32)
    short_valid = offsets[None, :] < short_lengths[:, None]
    short_init = (
        jnp.full((short_count, heads_dev, SLEN), NEG, jnp.float32),
        jnp.zeros((short_count, heads_dev, SLEN), jnp.float32),
        jnp.zeros((short_count, heads_dev, SLEN, HEAD_SIZE), jnp.float32),
    )
    short_state = attend(short_init, short_q, offsets, short_k, short_v, offsets, short_valid)
    short_out = (
        (short_state[2] / short_state[1][..., None])
        .astype(jnp.bfloat16)
        .transpose(0, 2, 1, 3)
        .reshape(short_count * SLEN, q_cols)
    )
    short_cache = lax.dynamic_slice_in_dim(
        jnp.concatenate([short_k, short_v], axis=-1), first_col, cache_cols, 2
    )
    attn = jnp.concatenate([long_out, short_out], axis=0)
    mixed = lax.psum_scatter(
        jnp.dot(attn, wo, preferred_element_type=jnp.float32).astype(jnp.bfloat16),
        "tp",
        scatter_dimension=0,
        tiled=True,
    ).astype(jnp.float32)
    residual = (states.astype(jnp.float32) + mixed).astype(jnp.bfloat16)
    piece = lax.all_gather(rms_scale(residual, mlp_gain), "tp", axis=0, tiled=True)
    gate = jnp.dot(piece, w_gate, preferred_element_type=jnp.float32)
    up_part = jnp.dot(piece, w_up, preferred_element_type=jnp.float32)
    hidden = (jax.nn.silu(gate) * up_part).astype(jnp.bfloat16)
    down = lax.psum_scatter(
        jnp.dot(hidden, w_down, preferred_element_type=jnp.float32).astype(jnp.bfloat16),
        "tp",
        scatter_dimension=0,
        tiled=True,
    ).astype(jnp.float32)
    updated = (residual.astype(jnp.float32) + down).astype(jnp.bfloat16)
    return (updated, long_cache, short_cache)


def solution(mesh):
    in_specs = (
        P(("ctx", "tp"), None),
        P("ctx"),
        P(),
        P(None, "tp"),
        P(),
        P("tp", None),
        P(),
        P(None, "tp"),
        P(None, "tp"),
        P("tp", None),
    )
    out_specs = (P(("ctx", "tp"), None), P(None, "ctx", "tp"), P("ctx", None, "tp"))
    return jax.shard_map(
        per_device, mesh=mesh, in_specs=in_specs, out_specs=out_specs, check_vma=False
    )
```

profile of v0, /device:TPU:2, one launch (start us, length us, event | category | flops | bytes accessed | tf_op | source)
XLA Modules:
  0.0 431.4 jit_solution(14815538953844404363)
XLA Ops:
  7.2 0.0 copy-start
  7.2 0.0 all-gather.3.cloned.1.call-start
  7.2 1.2 fusion.28
  8.4 1.7 fusion.30
  10.1 0.0 all-gather.3.cloned.1.call-update
  10.1 0.0 reduce-scatter.3.cloned.1.call-start
  10.2 0.6 and_select_fusion.1
  10.9 1.3 iota_compare_fusion.1
  12.1 0.1 add_bitcast_fusion
  12.2 1.2 broadcast_compare_fusion
  13.4 61.1 %all-gather.3.cloned.1.call-done = bf16[1024,2048]{1,0:T(8,128)(2,1)} async-done(((bf16[32,2048]{1,0:T(8,128)(2,1)}), bf16[1024,2048]{1,0:T(8,128)(2,1)}) %all-gather.3.cloned.1.call-update) | async-done | bytes 4194320 | tf_op jit(solution)/shard_map/all_gather | solution.py:101
  74.5 0.0 copy-done
  74.5 3.7 fusion.105
  78.2 0.1 reshape.518
  78.4 0.0 copy-done.6
  78.4 0.0 copy-start.9
  78.4 3.6 convolution_bitcast_fusion
  82.0 0.6 fusion.52
  82.7 0.1 reshape.517
  82.8 0.0 copy-start.5
  82.8 0.1 copy.51
  83.0 0.0 copy-done.9
  83.0 0.3 fusion.104
  83.3 0.1 fusion.36
  83.4 0.5 fusion.8
  83.9 0.1 copy.43
  84.0 0.0 copy-done.5
  84.0 27.9 %all_gather.13 = bf16[2,2,8,128,64]{3,4,1,0,2:T(8,128)(2,1)S(1)} all-gather(bf16[2,2,1,128,64]{3,4,1,0,2:T(8,128)(2,1)S(1)} %copy.33), channel_id=1, replica_groups=mesh['ctx'=8,'tp'=32] {'ctx'}, dimensions={2}, use_global_device_ids=true | all-gather | bytes 589824 | tf_op jit(solution)/shard_map/all_gather | solution.py:125
  111.9 0.3 copy.34
  112.2 30.0 %all_gather.14 = bf16[2,2,8,128,64]{3,4,1,0,2:T(8,128)(2,1)S(1)} all-gather(bf16[2,2,1,128,64]{3,4,1,0,2:T(8,128)(2,1)S(1)} %copy.36), channel_id=1, replica_groups=mesh['ctx'=8,'tp'=32] {'ctx'}, dimensions={2}, use_global_device_ids=true | all-gather | bytes 589824 | tf_op jit(solution)/shard_map/all_gather | solution.py:126
  142.2 0.3 copy.37
  142.6 1.0 reshape.515
  143.6 1.0 reshape.513
  144.6 2.4 fusion
  147.0 0.0 copy-done.1
  147.0 1.4 fusion.1
  148.4 0.0 copy-done.4
  148.4 0.0 copy-start.7
  148.4 1.1 fusion.17
  149.6 0.0 copy-done.7
  149.6 0.0 copy-start.2
  149.6 0.0 copy-start.8
  149.6 3.2 convolution_convert_fusion.1
  152.8 0.0 reduce-scatter.3.cloned.1.call-update
  152.8 0.0 all-gather.5.cloned.1.call-start
  152.9 99.4 %reduce-scatter.3.cloned.1.call-done = bf16[32,2048]{1,0:T(8,128)(2,1)} async-done(((bf16[1024,2048]{1,0:T(8,128)(2,1)}), bf16[32,2048]{1,0:T(8,128)(2,1)}) %reduce-scatter.3.cloned.1.call-update) | async-done | bytes 131088 | tf_op jit(solution)/shard_map/reduce_scatter | solution.py:181
  252.3 0.0 copy-done.2
  252.3 1.1 fusion.32
  253.3 0.0 copy-done.8
  253.3 1.7 fusion.34
  255.0 0.0 all-gather.5.cloned.1.call-update
  255.0 0.2 reduce-scatter.5.cloned.1.call-start
  255.3 58.1 %all-gather.5.cloned.1.call-done = bf16[1024,2048]{1,0:T(8,128)(2,1)} async-done(((bf16[32,2048]{1,0:T(8,128)(2,1)}), bf16[1024,2048]{1,0:T(8,128)(2,1)}) %all-gather.5.cloned.1.call-update) | async-done | bytes 4194320 | tf_op jit(solution)/shard_map/all_gather | solution.py:188
  313.3 4.8 %fusion.106 = f32[1024,176]{0,1:T(8,128)} fusion(bf16[1024,2048]{1,0:T(8,128)(2,1)} %all-gather.5.cloned.1.call-done, bf16[2048,176]{0,1:T(8,128)(2,1)} %param.17), kind=kOutput, calls=%fused_computation.156 | convolution fusion | flops 738197504 | bytes 5636096 | tf_op jit(solution)/shard_map/dot_general | solution.py:189
  318.2 7.5 %convolution_convert_fusion = bf16[1024,2048]{1,0:T(8,128)(2,1)} fusion(bf16[176,2048]{1,0:T(8,128)(2,1)} %param.19, bf16[1024,2048]{1,0:T(8,128)(2,1)} %all-gather.5.cloned.1.call-done, bf16[2048,176]{0,1:T(8,128)(2,1)} %param.18, f32[1024,176]{0,1:T(8,128)} %fusion.106), kind=kOutput, calls=%fused_computation.2 | convolution fusion | flops 1479573504 | bytes 10551296 | tf_op jit(solution)/shard_map/dot_general | solution.py:193
  325.6 0.0 reduce-scatter.5.cloned.1.call-update
  325.7 0.7 copy.47
  326.4 0.9 copy.46
  327.3 0.9 fusion.10
  328.2 0.6 reshape.519
  328.8 0.6 fusion.68
  329.5 93.7 %reduce-scatter.5.cloned.1.call-done = bf16[32,2048]{1,0:T(8,128)(2,1)} async-done(((bf16[1024,2048]{1,0:T(8,128)(2,1)}), bf16[32,2048]{1,0:T(8,128)(2,1)}) %reduce-scatter.5.cloned.1.call-update) | async-done | bytes 131088 | tf_op jit(solution)/shard_map/reduce_scatter | solution.py:192
  423.2 0.0 copy-done.3
  423.2 1.6 fusion.35
  (25 shorter events, 0.3 us)
Async XLA Ops:
  7.2 67.3 %copy-start = (bf16[2048,512]{1,0:T(8,128)(2,1)S(1)}, bf16[2048,512]{1,0:T(8,128)(2,1)}, u32[]{:S(2)}) copy-start(bf16[2048,512]{1,0:T(8,128)(2,1)} %param.14) | copy-start | bytes 6291460
  7.2 67.3 %all-gather.3.cloned.1.call-start = ((), (), s32[]{:S(2)}) async-start(), calls=%async_computation.2 | async-start | bytes 4325376 | tf_op jit(solution)/shard_map/all_gather | solution.py:101
  10.1 242.2 %reduce-scatter.3.cloned.1.call-start = ((), (), s32[]{:S(2)}) async-start(), calls=%async_computation.3 | async-start | bytes 4325376 | tf_op jit(solution)/shard_map/reduce_scatter | solution.py:181
  13.4 65.0 %copy-start.6 = (bf16[2048,64]{0,1:T(8,128)(2,1)S(1)}, bf16[2048,64]{0,1:T(8,128)(2,1)}, u32[]{:S(2)}) copy-start(bf16[2048,64]{0,1:T(8,128)(2,1)} %param.13) | copy-start | bytes 786436
  78.4 4.6 %copy-start.9 = (pred[8,64]{1,0:T(8,128)(4,1)S(1)}, pred[8,64]{1,0:T(8,128)(4,1)}, u32[]{:S(2)}) copy-start(pred[8,64]{1,0:T(8,128)(4,1)} %iota_compare_fusion.1) | copy-start | bytes 1540
  82.8 1.1 copy-start.5
  144.6 2.4 copy-start.1
  144.6 3.8 copy-start.4
  148.4 1.2 copy-start.7
  149.6 102.7 %copy-start.2 = (bf16[32,2048]{1,0:T(8,128)(2,1)S(1)}, bf16[32,2048]{1,0:T(8,128)(2,1)}, u32[]{:S(2)}) copy-start(bf16[32,2048]{1,0:T(8,128)(2,1)} %param.10) | copy-start | bytes 393220
  149.6 103.8 %copy-start.8 = (f32[2048]{0:T(1024)S(1)}, f32[2048]{0:T(1024)}, u32[]{:S(2)}) copy-start(f32[2048]{0:T(1024)} %param.16) | copy-start | bytes 24580
  152.8 160.5 %all-gather.5.cloned.1.call-start = ((), (), s32[]{:S(2)}) async-start(), calls=%async_computation.4 | async-start | bytes 4325376 | tf_op jit(solution)/shard_map/all_gather | solution.py:188
  255.0 168.2 %reduce-scatter.5.cloned.1.call-start = ((), (), s32[]{:S(2)}) async-start(), calls=%async_computation.5 | async-start | bytes 4325376 | tf_op jit(solution)/shard_map/reduce_scatter | solution.py:192
  325.6 97.6 %copy-start.3 = (bf16[32,2048]{1,0:T(8,128)(2,1)S(1)}, bf16[32,2048]{1,0:T(8,128)(2,1)}, u32[]{:S(2)}) copy-start(bf16[32,2048]{1,0:T(8,128)(2,1)} %reduce-scatter.3.cloned.1.call-done) | copy-start | bytes 393220
Sparse Core Ops, SparseCore 0:
  11.1 63.2 all-gather.2
  153.0 99.2 reduce-scatter.2
  255.7 57.5 all-gather.4
  325.8 97.4 reduce-scatter.4
where the time goes:
time: 432 us; the launch traced here: 431 us
  waiting for transfers between devices  312 us (72%)
  blocking collectives  57.9 us (13%)
  matrix products  28 us (6%)
  between operations  14.1 us (3%)
  other arithmetic  13.2 us (3%)
  local copies, waits for them, and re-layouts  5.59 us (1%)
    reduce_scatter x1, waiting for transfers between devices, per_device(): lax.psum_scatter(jnp.dot(attn, wo, preferred_element_type=jnp.float32).as...  99.4 us
    reduce_scatter x1, waiting for transfers between devices, per_device(): lax.psum_scatter(jnp.dot(hidden, w_down, preferred_element_type=jnp.float...  93.7 us
    all_gather x1, waiting for transfers between devices, per_device(): lax.all_gather(rms_scale(states, attn_gain), 'tp', axis=0, tiled=True)  61.1 us
    all_gather x1, waiting for transfers between devices, per_device(): lax.all_gather(rms_scale(residual, mlp_gain), 'tp', axis=0, tiled=True)  58.1 us
    all_gather x1, blocking collectives, per_device(): piece_v = lax.all_gather(long_v, 'ctx', axis=2, tiled=True)  30 us
    all_gather x1, blocking collectives, per_device(): piece_k = lax.all_gather(long_k, 'ctx', axis=2, tiled=True)  27.9 us
  transfers between devices with their start and end apart: 4, of which 4 were waited for; matrix products, arithmetic and copies ran while one was open for 2% of the time, Pallas kernels for 0%

commit v1 on v0

--- a/solution.py
+++ b/solution.py
@@ -2,6 +2,7 @@
 import jax.numpy as jnp
 from jax import lax
 from jax.sharding import PartitionSpec as P
+from jax.lax import all_to_all, axis_size
 
 KVH = 4
 HEAD_SIZE = 64
@@ -98,7 +99,15 @@
     first_col = tp_index * cache_cols - kv_group * pair_width
     positions = rank_positions(ctx_rank, rank_rows, block_len, long_rows, n_blocks)
     packed = project(
-        lax.all_gather(rms_scale(states, attn_gain), "tp", axis=0, tiled=True),
+        jnp.concatenate(
+            all_to_all(
+                jnp.stack(axis_size("tp") * [rms_scale(states, attn_gain)], axis=0),
+                axis_name="tp",
+                concat_axis=0,
+                split_axis=0,
+            ),
+            0,
+        ),
         positions,
         wq,
         wkv_head,

time: 432 us -> 478 us (1.11)
  waiting for transfers between devices: 312 us -> 344 us
  starting transfers between devices: 0.34 us -> 12.1 us
    all_to_all x0 -> x1, waiting for transfers between devices: none -> 93.6 us  [per_device(): all_to_all(jnp.stack(axis_size('tp') * [rms_scale(states, attn_gain)], ax...]
    all_gather x1 -> x0, waiting for transfers between devices: 61.1 us -> none  [per_device(): lax.all_gather(rms_scale(states, attn_gain), 'tp', axis=0, tiled=True)]
    all_to_all x0 -> x1, starting transfers between devices: none -> 11.7 us  [per_device(): all_to_all(jnp.stack(axis_size('tp') * [rms_scale(states, attn_gain)], ax...]
  transfers between devices with their start and end apart: 4 -> 4, of which waited for: 4 -> 4; matrix products, arithmetic and copies ran while one was open for 2% -> 1% of each run, Pallas kernels for 0% -> 0%
where the time goes in v1:
time: 478 us
  waiting for transfers between devices  344 us (72%)
  blocking collectives  57.7 us (12%)
  matrix products  29.3 us (6%)
  between operations  14.1 us (3%)
  other arithmetic  12.6 us (3%)
  starting transfers between devices  12.1 us (3%)
  local copies, waits for them, and re-layouts  8.09 us (2%)
    reduce_scatter x1, waiting for transfers between devices, per_device(): lax.psum_scatter(jnp.dot(attn, wo, preferred_element_type=jnp.float32).as...  98.7 us
    reduce_scatter x1, waiting for transfers between devices, per_device(): lax.psum_scatter(jnp.dot(hidden, w_down, preferred_element_type=jnp.float...  93.7 us
    all_to_all x1, waiting for transfers between devices, per_device(): all_to_all(jnp.stack(axis_size('tp') * [rms_scale(states, attn_gain)], ax...  93.6 us
    all_gather x1, waiting for transfers between devices, per_device(): lax.all_gather(rms_scale(residual, mlp_gain), 'tp', axis=0, tiled=True)  58 us
    all_gather x1, blocking collectives, per_device(): piece_v = lax.all_gather(long_v, 'ctx', axis=2, tiled=True)  30 us
    all_gather x1, blocking collectives, per_device(): piece_k = lax.all_gather(long_k, 'ctx', axis=2, tiled=True)  27.7 us
    all_to_all x1, starting transfers between devices, per_device(): all_to_all(jnp.stack(axis_size('tp') * [rms_scale(states, attn_gain)], ax...  11.7 us
  transfers between devices with their start and end apart: 4, of which 4 were waited for; matrix products, arithmetic and copies ran while one was open for 1% of the time, Pallas kernels for 0%

profile of v1, /device:TPU:2, one launch (start us, length us, event | category | flops | bytes accessed | tf_op | source)
XLA Modules:
  0.0 477.8 jit_solution(8010109845379656204)
XLA Ops:
  7.2 0.0 copy-start
  7.2 1.2 fusion.28
  8.4 1.0 fusion.30
  9.4 2.5 stack.5
  11.9 0.0 copy-start.9
  11.9 11.7 %all-to-all-start = ((bf16[32,32,2048]{2,1,0:T(8,128)(2,1)}), bf16[32,32,2048]{2,1,0:T(8,128)(2,1)}, u32[]{:S(2)}, u32[]{:S(2)}) async-start(bf16[32,32,2048]{2,1,0:T(8,128)(2,1)} %stack.5), calls=%async_computation | async-start | bytes 8388608 | tf_op jit(solution)/shard_map/all_to_all | solution.py:103
  23.6 0.0 reduce-scatter.3.cloned.1.call-start
  23.8 0.6 and_select_fusion.1
  24.4 0.0 copy-done.9
  24.4 0.6 iota_compare_fusion.1
  25.0 0.1 add_bitcast_fusion
  25.1 1.2 broadcast_compare_fusion
  26.3 93.6 %all-to-all-done = bf16[32,32,2048]{2,1,0:T(8,128)(2,1)} async-done(((bf16[32,32,2048]{2,1,0:T(8,128)(2,1)}), bf16[32,32,2048]{2,1,0:T(8,128)(2,1)}, u32[]{:S(2)}, u32[]{:S(2)}) %all-to-all-start) | async-done | bytes 4194336 | tf_op jit(solution)/shard_map/all_to_all | solution.py:103
  119.9 0.0 copy-done.6
  119.9 3.6 convolution_bitcast_fusion
  123.5 0.0 copy-done
  123.5 3.7 fusion.105
  127.2 0.1 reshape.524
  127.4 0.6 fusion.52
  128.1 0.1 reshape.523
  128.2 0.0 copy-start.5
  128.2 0.1 copy.51
  128.4 0.9 fusion.104
  129.3 0.8 fusion.36
  130.2 1.1 fusion.8
  131.3 0.1 copy.43
  131.4 0.0 copy-done.5
  131.4 27.7 %all_gather.9 = bf16[2,2,8,128,64]{3,4,1,0,2:T(8,128)(2,1)S(1)} all-gather(bf16[2,2,1,128,64]{3,4,1,0,2:T(8,128)(2,1)S(1)} %copy.33), channel_id=1, replica_groups=mesh['ctx'=8,'tp'=32] {'ctx'}, dimensions={2}, use_global_device_ids=true | all-gather | bytes 589824 | tf_op jit(solution)/shard_map/all_gather | solution.py:134
  159.2 0.3 copy.34
  159.5 30.0 %all_gather.10 = bf16[2,2,8,128,64]{3,4,1,0,2:T(8,128)(2,1)S(1)} all-gather(bf16[2,2,1,128,64]{3,4,1,0,2:T(8,128)(2,1)S(1)} %copy.36), channel_id=1, replica_groups=mesh['ctx'=8,'tp'=32] {'ctx'}, dimensions={2}, use_global_device_ids=true | all-gather | bytes 589824 | tf_op jit(solution)/shard_map/all_gather | solution.py:135
  189.5 0.3 copy.37
  189.8 1.0 reshape.521
  190.9 1.0 reshape.519
  191.9 2.4 fusion
  194.3 0.0 copy-done.1
  194.3 1.4 fusion.1
  195.7 0.0 copy-done.4
  195.7 0.0 copy-start.7
  195.7 1.1 fusion.17
  196.8 0.0 copy-done.7
  196.9 0.0 copy-start.2
  196.9 0.0 copy-start.8
  196.9 3.2 convolution_convert_fusion.1
  200.1 0.0 reduce-scatter.3.cloned.1.call-update
  200.1 0.0 all-gather.2.cloned.1.call-start
  200.2 98.7 %reduce-scatter.3.cloned.1.call-done = bf16[32,2048]{1,0:T(8,128)(2,1)} async-done(((bf16[1024,2048]{1,0:T(8,128)(2,1)}), bf16[32,2048]{1,0:T(8,128)(2,1)}) %reduce-scatter.3.cloned.1.call-update) | async-done | bytes 131088 | tf_op jit(solution)/shard_map/reduce_scatter | solution.py:190
  298.9 0.0 copy-done.2
  298.9 1.1 fusion.32
  299.9 0.0 copy-done.8
  299.9 1.7 fusion.34
  301.6 0.0 all-gather.2.cloned.1.call-update
  301.6 0.2 reduce-scatter.5.cloned.1.call-start
  301.8 58.0 %all-gather.2.cloned.1.call-done = bf16[1024,2048]{1,0:T(8,128)(2,1)} async-done(((bf16[32,2048]{1,0:T(8,128)(2,1)}), bf16[1024,2048]{1,0:T(8,128)(2,1)}) %all-gather.2.cloned.1.call-update) | async-done | bytes 4194320 | tf_op jit(solution)/shard_map/all_gather | solution.py:197
  359.8 4.8 %fusion.106 = f32[1024,176]{0,1:T(8,128)} fusion(bf16[1024,2048]{1,0:T(8,128)(2,1)} %all-gather.2.cloned.1.call-done, bf16[2048,176]{0,1:T(8,128)(2,1)} %param.17), kind=kOutput, calls=%fused_computation.156 | convolution fusion | flops 738197504 | bytes 5636096 | tf_op jit(solution)/shard_map/dot_general | solution.py:198
  364.6 7.5 %convolution_convert_fusion = bf16[1024,2048]{1,0:T(8,128)(2,1)} fusion(bf16[176,2048]{1,0:T(8,128)(2,1)} %param.19, bf16[1024,2048]{1,0:T(8,128)(2,1)} %all-gather.2.cloned.1.call-done, bf16[2048,176]{0,1:T(8,128)(2,1)} %param.18, f32[1024,176]{0,1:T(8,128)} %fusion.106), kind=kOutput, calls=%fused_computation.2 | convolution fusion | flops 1479573504 | bytes 10551296 | tf_op jit(solution)/shard_map/dot_general | solution.py:202
  372.1 0.0 reduce-scatter.5.cloned.1.call-update
  372.1 0.7 copy.47
  372.8 0.9 copy.46
  373.8 0.9 fusion.10
  374.7 0.6 reshape.525
  375.3 0.6 fusion.68
  376.0 93.7 %reduce-scatter.5.cloned.1.call-done = bf16[32,2048]{1,0:T(8,128)(2,1)} async-done(((bf16[1024,2048]{1,0:T(8,128)(2,1)}), bf16[32,2048]{1,0:T(8,128)(2,1)}) %reduce-scatter.5.cloned.1.call-update) | async-done | bytes 131088 | tf_op jit(solution)/shard_map/reduce_scatter | solution.py:201
  469.6 0.0 copy-done.3
  469.6 1.6 fusion.35
  (25 shorter events, 0.3 us)
Async XLA Ops:
  7.2 116.3 %copy-start = (bf16[2048,512]{1,0:T(8,128)(2,1)S(1)}, bf16[2048,512]{1,0:T(8,128)(2,1)}, u32[]{:S(2)}) copy-start(bf16[2048,512]{1,0:T(8,128)(2,1)} %param.14) | copy-start | bytes 6291460
  11.9 12.5 %copy-start.9 = (s32[8]{0:T(128)S(1)}, s32[8]{0:T(128)}, u32[]{:S(2)}) copy-start(s32[8]{0:T(128)} %param.11) | copy-start | bytes 100
  11.9 108.0 %copy-start.6 = (bf16[2048,64]{0,1:T(8,128)(2,1)S(1)}, bf16[2048,64]{0,1:T(8,128)(2,1)}, u32[]{:S(2)}) copy-start(bf16[2048,64]{0,1:T(8,128)(2,1)} %param.13) | copy-start | bytes 786436
  11.9 108.0 %all-to-all-start = ((bf16[32,32,2048]{2,1,0:T(8,128)(2,1)}), bf16[32,32,2048]{2,1,0:T(8,128)(2,1)}, u32[]{:S(2)}, u32[]{:S(2)}) async-start(bf16[32,32,2048]{2,1,0:T(8,128)(2,1)} %stack.5), calls=%async_computation | async-start | bytes 8388608 | tf_op jit(solution)/shard_map/all_to_all | solution.py:103
  23.6 275.2 %reduce-scatter.3.cloned.1.call-start = ((), (), s32[]{:S(2)}) async-start(), calls=%async_computation.3 | async-start | bytes 4325376 | tf_op jit(solution)/shard_map/reduce_scatter | solution.py:190
  128.2 3.2 copy-start.5
  191.9 2.4 copy-start.1
  191.9 3.8 copy-start.4
  195.7 1.2 copy-start.7
  196.9 102.0 %copy-start.2 = (bf16[32,2048]{1,0:T(8,128)(2,1)S(1)}, bf16[32,2048]{1,0:T(8,128)(2,1)}, u32[]{:S(2)}) copy-start(bf16[32,2048]{1,0:T(8,128)(2,1)} %param.10) | copy-start | bytes 393220
  196.9 103.1 %copy-start.8 = (f32[2048]{0:T(1024)S(1)}, f32[2048]{0:T(1024)}, u32[]{:S(2)}) copy-start(f32[2048]{0:T(1024)} %param.16) | copy-start | bytes 24580
  200.1 159.7 %all-gather.2.cloned.1.call-start = ((), (), s32[]{:S(2)}) async-start(), calls=%async_computation.4 | async-start | bytes 4325376 | tf_op jit(solution)/shard_map/all_gather | solution.py:197
  301.6 168.0 %reduce-scatter.5.cloned.1.call-start = ((), (), s32[]{:S(2)}) async-start(), calls=%async_computation.5 | async-start | bytes 4325376 | tf_op jit(solution)/shard_map/reduce_scatter | solution.py:201
  372.1 97.6 %copy-start.3 = (bf16[32,2048]{1,0:T(8,128)(2,1)S(1)}, bf16[32,2048]{1,0:T(8,128)(2,1)}, u32[]{:S(2)}) copy-start(bf16[32,2048]{1,0:T(8,128)(2,1)} %reduce-scatter.3.cloned.1.call-done) | copy-start | bytes 393220
Sparse Core Ops, SparseCore 0:
  200.2 98.5 reduce-scatter.2
  302.3 57.4 all-gather.1
  372.2 97.3 reduce-scatter.4
